TPU v7x, 32 devices: a whole 2x2x4 slice. The times are simulated.
32 devices in a mesh: px: 4 (over y, x), py: 8 (over z, core).
Axes of the slice: x: 2, y: 2, z: 4, core: 2. Of those that a mesh axis runs over, the one named last changes fastest.
Arguments:
- residual: float32 [10, 2048, 2048], P(None, 'py', 'px'), may hold values from -6 to 6
- lambda_x: float32 [2048], P('px'), may hold values from 0.1 to 4
- lambda_y: float32 [2048], P('py'), may hold values from 0.1 to 4
- coupling: float32 [9], replicated, may hold values from 0.2 to 2
- layer_shift: float32 [10], replicated, may hold values from 0.05 to 1
- left_x: bfloat16 [2048, 2048], P(None, 'px'), may hold values from -0.125 to 0.125
- left_y: bfloat16 [2048, 2048], P('py'), may hold values from -0.125 to 0.125
- right_y: bfloat16 [2048, 2048], P('py'), may hold values from -0.125 to 0.125
- right_x: bfloat16 [2048, 2048], P(None, 'px'), may hold values from -0.125 to 0.125
- regime_code: int32 [10, 2048, 2048], P(None, 'py', 'px'), may hold values from 0 to 3
- upwind_flag: int32 [2, 10, 2048, 2048], P(None, None, 'py', 'px'), may hold values from 0 to 1
- mobility_table: float32 [4], replicated, may hold values from 0.3 to 3
Outputs:
- correction: float32 [10, 2048, 2048], P(None, 'py', 'px')
- balance: float32 [10, 2048, 2048], P(None, 'py', 'px')
Inputs may be any that keep to these rules, and one draw needn't show every extreme that they name: `regime_code`: a regime number of each cell.
All inputs are finite; a program needn't handle non-finite values.
Results may differ from a plain program's by a relative error of at most 0.0057.
Values may be sent and summed in bfloat16 or wider, within the bound.
No kernel may reach another device: no remote copies, remote signals or barrier semaphores. Data moves between devices by JAX's collectives and lax.ppermute only.
A program may use at most 192 MiB of HBM per device.

v0:
```python
import jax
import jax.numpy as jnp
from jax import lax
from jax.sharding import PartitionSpec as P


def with_halo(block, sides, width):
    for axis, dim in sides:
        count = lax.axis_size(axis)
        forward = [(i, i + 1) for i in range(count - 1)]
        backward = [(target, source) for source, target in forward]
        low = lax.ppermute(
            lax.slice_in_dim(block, block.shape[dim] - width, None, axis=dim), axis, forward
        )
        high = lax.ppermute(lax.slice_in_dim(block, 0, width, axis=dim), axis, backward)
        block = jnp.concatenate([low, block, high], axis=dim)
    return block


def thomas_solve(rhs, lambda_x, lambda_y, coupling, layer_shift):
    layers = rhs.shape[0]
    mode_sum = lambda_y[:, None] + lambda_x[None, :]
    ratios = []
    partial_values = []
    for layer_index in range(layers):
        diagonal = mode_sum + layer_shift[layer_index]
        if layer_index > 0:
            diagonal = diagonal + coupling[layer_index - 1]
        if layer_index < layers - 1:
            diagonal = diagonal + coupling[layer_index]
        if layer_index == 0:
            pivots = diagonal
            solved = rhs[0] / pivots
        else:
            pivots = diagonal + coupling[layer_index - 1] * ratios[-1]
            solved = (rhs[layer_index] + coupling[layer_index - 1] * partial_values[-1]) / pivots
        partial_values.append(solved)
        if layer_index < layers - 1:
            ratios.append(-coupling[layer_index] / pivots)
    results = [partial_values[layers - 1]]
    for layer_index in range(layers - 2, -1, -1):
        results.append(partial_values[layer_index] - ratios[layer_index] * results[-1])
    return jnp.stack(results[::-1])


def shards(
    residual,
    lambda_x,
    lambda_y,
    coupling,
    layer_shift,
    left_x,
    left_y,
    right_y,
    right_x,
    regime_code,
    upwind_flag,
    mobility_table,
):
    count_y = lax.axis_size("py")
    rounded = residual.astype(jnp.bfloat16)
    spectral_x = jnp.einsum(
        "zyx,xi->zyi",
        lax.all_gather(rounded, "px", axis=2, tiled=True),
        left_x,
        preferred_element_type=jnp.float32,
    ).astype(jnp.bfloat16)
    pencil = lax.all_to_all(spectral_x, "py", 2, 1, tiled=True)
    modes = pencil.shape[2]
    spectral = jnp.einsum(
        "jy,zyi->zji",
        lax.all_gather(left_y, "py", axis=0, tiled=True),
        pencil,
        preferred_element_type=jnp.float32,
    )
    own_x = lax.dynamic_slice_in_dim(lambda_x, lax.axis_index("py") * modes, modes)
    all_y = lax.all_gather(lambda_y, "py", axis=0, tiled=True)
    solved = thomas_solve(spectral, own_x, all_y, coupling, layer_shift).astype(jnp.bfloat16)
    back_pencil = jnp.einsum(
        "yj,zji->zyi",
        lax.all_gather(right_y, "py", axis=0, tiled=True),
        solved,
        preferred_element_type=jnp.float32,
    ).astype(jnp.bfloat16)
    back_y = lax.all_to_all(back_pencil, "py", 1, 2, tiled=True)
    del count_y
    mobility = jnp.zeros(regime_code.shape, jnp.float32)
    for regime in range(mobility_table.shape[0]):
        mobility = jnp.where(regime_code == regime, mobility_table[regime], mobility)
    correction = jnp.einsum(
        "zyi,ix->zyx",
        lax.all_gather(back_y, "px", axis=2, tiled=True),
        right_x,
        preferred_element_type=jnp.float32,
    )
    width_x = correction.shape[2]
    width_y = correction.shape[1]
    stacked = jnp.stack(
        [
            correction,
            mobility,
            upwind_flag[0].astype(jnp.float32),
            upwind_flag[1].astype(jnp.float32),
        ]
    )
    extended = with_halo(stacked, (("px", 3), ("py", 2)), 1)
    press_x = extended[0][:, 1:-1, :]
    mobil_x = extended[1][:, 1:-1, :]
    flags_x = extended[2][:, 1:-1, :]
    upwind_x = jnp.where(flags_x[:, :, :-1] > 0.5, mobil_x[:, :, :-1], mobil_x[:, :, 1:])
    flux_x = upwind_x * (press_x[:, :, :-1] - press_x[:, :, 1:])
    faces_x = lax.axis_index("px") * width_x + jnp.arange(width_x + 1, dtype=jnp.int32)
    valid_x = (faces_x >= 1) & (faces_x <= width_x * lax.axis_size("px") - 1)
    flux_x = jnp.where(valid_x[None, None, :], flux_x, 0.0)
    net_x = flux_x[:, :, 1:] - flux_x[:, :, :-1]
    press_y = extended[0][:, :, 1:-1]
    mobil_y = extended[1][:, :, 1:-1]
    flags_y = extended[3][:, :, 1:-1]
    upwind_y = jnp.where(flags_y[:, :-1, :] > 0.5, mobil_y[:, :-1, :], mobil_y[:, 1:, :])
    flux_y = upwind_y * (press_y[:, :-1, :] - press_y[:, 1:, :])
    faces_y = lax.axis_index("py") * width_y + jnp.arange(width_y + 1, dtype=jnp.int32)
    valid_y = (faces_y >= 1) & (faces_y <= width_y * lax.axis_size("py") - 1)
    flux_y = jnp.where(valid_y[None, :, None], flux_y, 0.0)
    net_y = flux_y[:, 1:, :] - flux_y[:, :-1, :]
    balance = net_x + net_y
    return (correction, balance)


def solution(mesh):
    return jax.shard_map(
        shards,
        mesh=mesh,
        in_specs=(
            P(None, "py", "px"),
            P("px"),
            P("py"),
            P(),
            P(),
            P(None, "px"),
            P("py", None),
            P("py", None),
            P(None, "px"),
            P(None, "py", "px"),
            P(None, None, "py", "px"),
            P(),
        ),
        out_specs=(P(None, "py", "px"), P(None, "py", "px")),
        check_vma=False,
    )
```

profile of v0, /device:TPU:3, one launch (start us, length us, event | category | flops | bytes accessed | tf_op | source)
XLA Modules:
  0.0 748.3 jit_solution(3291203513705140137)
XLA Ops:
  13.2 104.8 %all-gather.6.cloned.1.call-done = bf16[10,256,2048]{2,1,0:T(8,128)(2,1)} async-done(((bf16[10,256,512]{2,1,0:T(8,128)(2,1)}), bf16[10,256,2048]{2,1,0:T(8,128)(2,1)}) %all-gather.6.cloned.1.call-update) | async-done | bytes 10485776 | tf_op jit(solution)/shard_map/all_gather | solution.py:64
  118.0 10.8 %fusion.22 = bf16[10,256,512]{2,1,0:T(8,128)(2,1)} fusion(bf16[10,256,2048]{2,1,0:T(8,128)(2,1)} %all-gather.6.cloned.1.call-done, bf16[2048,512]{1,0:T(8,128)(2,1)S(1)} %copy-done), kind=kOutput, calls=%fused_computation.46 | convolution fusion | flops 5370019840 | bytes 15204352 | tf_op jit(solution)/shard_map/zyx,xi->zyi/dot_general | solution.py:62
  128.9 7.6 %copy.29 = bf16[10,256,512]{1,0,2:T(8,128)(2,1)} copy(bf16[10,256,512]{2,1,0:T(8,128)(2,1)} %fusion.22) | data formatting | bytes 5242880 | tf_op jit(solution)/shard_map/convert_element_type | solution.py:67
  136.5 5.5 all-to-all-start
  149.0 121.9 %all-gather = f32[8,1,256]{2,1,0:T(1,128)S(1)} all-gather(f32[1,1,256]{2,1,0:T(1,128)S(1)} %bitcast.92), channel_id=1, replica_groups=mesh['px'=4,'py'=8] {'py'}, dimensions={0}, use_global_device_ids=true | all-gather | bytes 9216 | tf_op jit(solution)/shard_map/all_gather | solution.py:77
  271.5 26.8 %all-to-all-done = bf16[10,256,512]{1,0,2:T(8,128)(2,1)} async-done(((bf16[10,256,512]{1,0,2:T(8,128)(2,1)}), bf16[10,256,512]{1,0,2:T(8,128)(2,1)}, u32[]{:S(2)}, u32[]{:S(2)}) %all-to-all-start) | async-done | bytes 2621472 | tf_op jit(solution)/shard_map/all_to_all | solution.py:68
  298.4 5.3 copy.31
  303.7 5.7 all_to_all.29
  309.4 9.0 %fusion.9 = f32[10,2048,64]{1,2,0:T(8,128)S(1)} fusion(bf16[10,2048,64]{1,2,0:T(8,128)(2,1)} %all_to_all.29, bf16[2048,2048]{1,0:T(8,128)(2,1)} %all-gather.8.cloned.1.call-done), kind=kOutput, calls=%fused_computation.29 | convolution fusion | flops 5368709120 | bytes 16252928 | tf_op jit(solution)/shard_map/jy,zyi->zji/dot_general | solution.py:70
  318.4 14.9 %fusion.70 = (bf16[10,2048,64]{1,2,0:T(8,128)(2,1)}, bf16[1,2048,64]{1,2,0:T(8,128)(2,1)S(1)}, f32[1,2048,64]{1,2,0:T(8,128)S(1)}, f32[1,2048,64]{1,2,0:T(8,128)...) fusion(f32[]{:T(128)S(6)} %neg.27, f32[]{:T(128)} %bitcast.9, ...), kind=kLoop, calls=%fused_computation.110 | loop fusion | flops 13631487 | bytes 8921456
  334.1 4.8 convert_dynamic-update-slice_fusion.7
  339.6 7.6 %convert_dynamic-update-slice_fusion.5 = bf16[10,2048,64]{1,2,0:T(8,128)(2,1)} fusion(bf16[10,2048,64]{1,2,0:T(8,128)(2,1)} %convert_dynamic-update-slice_fusion.6, f32[1,2048,64]{1,2,0:T(8,128)S(1)} %get-tuple-element.8, f32[1,2048,64]{1,2,0:T(8,128)S(1)} %get-tuple-element.5, f32[]{:T(128)} %bitcast.8, f32[]{:T(128)S(6)} %neg.27, f32[]{:T(128)} %bitcast.9, ...), kind=kLoop, calls=%fused_computation.116 | loop fusion | flops 4063232 | bytes 1324308
  348.0 10.4 %convert_dynamic-update-slice_fusion.3 = bf16[10,2048,64]{1,2,0:T(8,128)(2,1)} fusion(bf16[10,2048,64]{1,2,0:T(8,128)(2,1)} %convert_dynamic-update-slice_fusion.4, f32[1,2048,64]{1,2,0:T(8,128)S(1)} %get-tuple-element.7, f32[1,2048,64]{1,2,0:T(8,128)S(1)} %get-tuple-element.6, f32[]{:T(128)} %bitcast.8, f32[]{:T(128)S(6)} %neg.27, f32[]{:T(128)} %bitcast.9, ...), kind=kLoop, calls=%fused_computation.114 | loop fusion | flops 5636096 | bytes 1326364
  359.1 14.0 %convert_dynamic-update-slice_fusion.1 = bf16[10,2048,64]{1,2,0:T(8,128)(2,1)} fusion(bf16[10,2048,64]{1,2,0:T(8,128)(2,1)} %convert_dynamic-update-slice_fusion.2, f32[]{:T(128)} %bitcast.8, f32[]{:T(128)S(6)} %neg.27, f32[]{:T(128)} %bitcast.9, f32[]{:T(128)} %bitcast.10, f32[]{:T(128)S(6)} %neg.28, f32[]{:T(128)} %bitcast.11, f32[]{:T(128)} %bitcast.12, ...), kind=kLoop, calls=%fused_computation.112 | loop fusion | flops 8912896 | bytes 2377508
  373.1 14.0 %convert_dynamic-update-slice_fusion = bf16[10,2048,64]{1,2,0:T(8,128)(2,1)} fusion(bf16[10,2048,64]{1,2,0:T(8,128)(2,1)} %convert_dynamic-update-slice_fusion.1, f32[]{:T(128)} %bitcast.8, f32[]{:T(128)S(6)} %neg.27, f32[]{:T(128)} %bitcast.9, f32[]{:T(128)} %bitcast.10, f32[]{:T(128)S(6)} %neg.28, f32[]{:T(128)} %bitcast.11, f32[]{:T(128)} %bitcast.12, ...), kind=kLoop, calls=%fused_computation.111 | loop fusion | flops 8650752 | bytes 2377508 | tf_op jit(solution)/shard_map/stack | solution.py:43
  387.1 10.7 %fusion.15 = bf16[10,2048,64]{1,2,0:T(8,128)(2,1)} fusion(bf16[10,2048,64]{1,2,0:T(8,128)(2,1)} %convert_dynamic-update-slice_fusion, bf16[2048,2048]{1,0:T(8,128)(2,1)} %all-gather.10.cloned.1.call-done), kind=kOutput, calls=%fused_computation.31 | convolution fusion | flops 5370019840 | bytes 13631488 | tf_op jit(solution)/shard_map/yj,zji->zyi/dot_general | solution.py:79
  397.8 10.4 %copy.32 = bf16[10,2048,64]{2,0,1:T(8,128)(2,1)} copy(bf16[10,2048,64]{1,2,0:T(8,128)(2,1)} %fusion.15) | data formatting | bytes 5242880 | tf_op jit(solution)/shard_map/convert_element_type | solution.py:84
  408.2 9.0 %reshape.799 = bf16[8,2,81920]{2,1,0:T(2,128)(2,1)} reshape(bf16[2048,10,64]{2,1,0:T(8,128)(2,1)} %bitcast.83) | data formatting | bytes 5242880
  417.2 66.5 %all_to_all.36 = bf16[8,2,81920]{2,1,0:T(2,128)(2,1)} all-to-all(bf16[8,2,81920]{2,1,0:T(2,128)(2,1)} %reshape.799), channel_id=1, replica_groups=mesh['px'=4,'py'=8] {'py'}, dimensions={0} | all-to-all | bytes 5242880 | tf_op jit(solution)/shard_map/all_to_all | solution.py:85
  483.7 8.9 %reshape.800 = bf16[2048,10,64]{2,1,0:T(8,128)(2,1)} reshape(bf16[8,2,81920]{2,1,0:T(2,128)(2,1)} %all_to_all.36) | data formatting | bytes 5242880
  492.6 9.1 %copy.34 = bf16[10,256,8,64]{1,3,2,0:T(8,128)(2,1)} copy(bf16[10,256,8,64]{3,0,1,2:T(8,128)(2,1)} %bitcast.84) | data formatting | bytes 5242880 | tf_op jit(solution)/shard_map/all_to_all | solution.py:85
  506.8 9.1 %select_bitcast_fusion = f32[1,10,256,512]{3,2,1,0:T(8,128)} fusion(s32[10,256,512]{2,1,0:T(8,128)} %param.21, f32[]{:T(128)} %bitcast.38, f32[]{:T(128)} %bitcast.37, f32[]{:T(128)} %bitcast.36, f32[]{:T(128)} %bitcast.35), kind=kLoop, calls=%fused_computation.28 | loop fusion | flops 10485760 | bytes 10485776 | tf_op jit(solution)/shard_map/stack | solution.py:98
  515.8 10.4 %slice_convert_fusion.1 = (f32[1,10,256,512]{3,2,1,0:T(8,128)}, f32[1,10,256,512]{3,2,1,0:T(8,128)}) fusion(s32[2,10,256,512]{3,2,1,0:T(8,128)} %param.22), kind=kLoop, calls=%fused_computation.27 | loop fusion | flops 2621440 | bytes 20971520 | tf_op jit(solution)/shard_map/convert_element_type | solution.py:102
  526.2 83.4 %all-gather.12.cloned.1.call-done = bf16[10,256,2048]{2,1,0:T(8,128)(2,1)} async-done(((bf16[10,256,512]{2,1,0:T(8,128)(2,1)}), bf16[10,256,2048]{2,1,0:T(8,128)(2,1)}) %all-gather.12.cloned.1.call-update) | async-done | bytes 10485776 | tf_op jit(solution)/shard_map/all_gather | solution.py:92
  609.6 8.5 %fusion.18 = f32[10,256,512]{2,1,0:T(8,128)S(1)} fusion(bf16[10,256,2048]{2,1,0:T(8,128)(2,1)} %all-gather.12.cloned.1.call-done, bf16[2048,512]{1,0:T(8,128)(2,1)S(1)} %copy-done.14), kind=kOutput, calls=%fused_computation.42 | convolution fusion | flops 5368709120 | bytes 17825792 | tf_op jit(solution)/shard_map/zyi,ix->zyx/dot_general | solution.py:90
  618.2 5.9 pad_maximum_fusion.4
  644.9 5.4 collective-permute-start.2
  656.3 27.9 %pad_maximum_fusion = f32[4,10,258,514]{3,2,1,0:T(8,128)} fusion(f32[4,10,1,514]{3,2,1,0:T(1,128)S(1)} %collective-permute-done.3, f32[4,10,256,1]{3,2,1,0:T(8,128)S(1)} %copy-done.8, f32[1,10,256,512]{3,2,1,0:T(8,128)} %get-tuple-element.19, f32[1,10,256,512]{3,2,1,0:T(8,128)S(1)} %bitcast.79, f32[1,10,256,512]{3,2,1,0:T(8,128)} %select_bitcast_fusion, ...), kind=kLoop, calls=%fused_computation | loop fusion | flops 37131360 | bytes 42435840 | tf_op jit(solution)/shard_map/concatenate | solution.py:16
  684.2 18.6 %slice_bitcast_fusion.3 = (f32[10,258,514]{2,1,0:T(8,128)}, f32[10,258,514]{2,1,0:T(8,128)}, f32[10,258,514]{2,1,0:T(8,128)}, f32[10,258,514]{2,1,0:T(8,128)}) fusion(f32[4,10,258,514]{3,2,1,0:T(8,128)} %pad_maximum_fusion), kind=kLoop, calls=%fused_computation.8 | loop fusion | bytes 42435840 | tf_op jit(solution)/shard_map/squeeze | solution.py:109
  702.7 14.9 %fusion.5 = f32[10,256,513]{2,1,0:T(8,128)} fusion(f32[10,258,514]{2,1,0:T(8,128)} %get-tuple-element.14, f32[10,258,514]{2,1,0:T(8,128)} %get-tuple-element.15, f32[10,258,514]{2,1,0:T(8,128)} %get-tuple-element.12, pred[513]{0:T(1024)(128)(4,1)S(1)} %fusion.73), kind=kLoop, calls=%fused_computation.11 | loop fusion | flops 6566400 | bytes 31519232 | tf_op jit(solution)/shard_map/jit(_where)/select_n | solution.py:114
  719.6 10.7 %fusion.7 = f32[10,257,512]{2,1,0:T(8,128)} fusion(f32[10,258,514]{2,1,0:T(8,128)S(1)} %copy-done.2, f32[10,258,514]{2,1,0:T(8,128)S(1)} %copy-done.3, f32[10,258,514]{2,1,0:T(8,128)} %get-tuple-element.13, pred[257]{0:T(512)(128)(4,1)S(1)} %fusion.76), kind=kLoop, calls=%fused_computation.16 | loop fusion | flops 6579200 | bytes 31580416 | tf_op jit(solution)/shard_map/jit(_where)/select_n | solution.py:123
  730.3 11.2 %fusion.8 = f32[10,256,512]{2,1,0:T(8,128)} fusion(f32[10,257,512]{2,1,0:T(8,128)} %fusion.7, f32[10,256,513]{2,1,0:T(8,128)} %fusion.5), kind=kLoop, calls=%fused_computation.20 | loop fusion | flops 3932160 | bytes 26214400 | tf_op jit(solution)/shard_map/add | solution.py:125
  (69 shorter events, 44.8 us)
Async XLA Ops:
  7.2 110.8 %copy-start = (bf16[2048,512]{1,0:T(8,128)(2,1)S(1)}, bf16[2048,512]{1,0:T(8,128)(2,1)}, u32[]{:S(2)}) copy-start(bf16[2048,512]{1,0:T(8,128)(2,1)} %param.17) | copy-start | bytes 6291460
  7.2 110.8 %all-gather.6.cloned.1.call-start = ((), (), s32[]{:S(2)}) async-start(), calls=%async_computation.2 | async-start | bytes 13107200 | tf_op jit(solution)/shard_map/all_gather | solution.py:64
  11.7 297.7 %all-gather.8.cloned.1.call-start = ((), (), s32[]{:S(2)}) async-start(), calls=%async_computation.3 | async-start | bytes 9437184 | tf_op jit(solution)/shard_map/all_gather | solution.py:72
  12.5 374.6 %all-gather.10.cloned.1.call-start = ((), (), s32[]{:S(2)}) async-start(), calls=%async_computation.4 | async-start | bytes 9437184 | tf_op jit(solution)/shard_map/all_gather | solution.py:81
  136.5 5.5 copy-start.11
  136.5 12.5 %copy-start.13 = (f32[256]{0:T(256)S(1)}, f32[256]{0:T(256)}, u32[]{:S(2)}) copy-start(f32[256]{0:T(256)} %param.14) | copy-start | bytes 3076
  136.5 134.4 %copy-start.10 = (f32[10]{0:T(128)S(1)}, f32[10]{0:T(128)}, u32[]{:S(2)}) copy-start(f32[10]{0:T(128)} %param.16) | copy-start | bytes 124
  136.5 161.9 %all-to-all-start = ((bf16[10,256,512]{1,0,2:T(8,128)(2,1)}), bf16[10,256,512]{1,0,2:T(8,128)(2,1)}, u32[]{:S(2)}, u32[]{:S(2)}) async-start(bf16[10,256,512]{1,0,2:T(8,128)(2,1)} %copy.29), calls=%async_computation | async-start | bytes 8388608 | tf_op jit(solution)/shard_map/all_to_all | solution.py:68
  142.0 467.6 %all-gather.12.cloned.1.call-start = ((), (), s32[]{:S(2)}) async-start(), calls=%async_computation.5 | async-start | bytes 13107200 | tf_op jit(solution)/shard_map/all_gather | solution.py:92
  501.7 4.4 copy-start.12
  515.8 93.8 %copy-start.14 = (bf16[2048,512]{1,0:T(8,128)(2,1)S(1)}, bf16[2048,512]{1,0:T(8,128)(2,1)}, u32[]{:S(2)}) copy-start(bf16[2048,512]{1,0:T(8,128)(2,1)} %param.20) | copy-start | bytes 6291460
  609.6 8.5 %copy-start.4 = (f32[1,10,256,512]{3,2,1,0:T(8,128)S(1)}, f32[1,10,256,512]{3,2,1,0:T(8,128)}, u32[]{:S(2)}) copy-start(f32[1,10,256,512]{3,2,1,0:T(8,128)} %get-tuple-element.18) | copy-start | bytes 15728644
  609.6 8.5 %copy-start.5 = (f32[1,10,256,512]{3,2,1,0:T(8,128)S(1)}, f32[1,10,256,512]{3,2,1,0:T(8,128)}, u32[]{:S(2)}) copy-start(f32[1,10,256,512]{3,2,1,0:T(8,128)} %get-tuple-element.19) | copy-start | bytes 15728644
  609.6 8.6 %copy-start.6 = (f32[1,10,256,512]{3,2,1,0:T(8,128)S(1)}, f32[1,10,256,512]{3,2,1,0:T(8,128)}, u32[]{:S(2)}) copy-start(f32[1,10,256,512]{3,2,1,0:T(8,128)} %select_bitcast_fusion) | copy-start | bytes 15728644
  618.1 6.0 copy-start.9
  627.4 8.6 %collective-permute-start = (f32[4,10,256,1]{2,0,3,1:T(4,128)S(1)}, f32[4,10,256,1]{2,0,3,1:T(4,128)S(1)}, u32[]{:S(2)}, u32[]{:S(2)}) collective-permute-start(f32[4,10,256,1]{2,0,3,1:T(4,128)S(1)} %copy.36), channel_id=1, source_target_pairs={{0,8},{8,16},{16,24},{1,9},{9,17},{17,25},{2,10},{10,18},{18,26},{... | collective-permute-start | bytes 122888 | tf_op jit(solution)/shard_map/ppermute | solution.py:12
  633.9 5.6 collective-permute-start.1
  639.5 16.8 %slice-start = ((s8[5242880]{0:T(1024)(128)(4,1)}), s8[1048576]{0:T(1024)(128)(4,1)S(1)}, s32[]{:S(2)}) async-start(s8[5242880]{0:T(1024)(128)(4,1)} %bitcast.78), calls=%async_computation.6 | async-start | bytes 2097152
  642.6 13.7 %slice-start.1 = ((s8[5242880]{0:T(1024)(128)(4,1)}), s8[4194304]{0:T(1024)(128)(4,1)S(1)}, s32[]{:S(2)}) async-start(s8[5242880]{0:T(1024)(128)(4,1)} %bitcast.78), calls=%async_computation.7 | async-start | bytes 8388608
  642.6 13.7 %copy-start.7 = (f32[4,10,256,1]{3,2,1,0:T(8,128)S(1)}, f32[4,10,256,1]{3,2,1,0:T(8,128)}, u32[]{:S(2)}) copy-start(f32[4,10,256,1]{3,2,1,0:T(8,128)} %copy.38) | copy-start | bytes 122884
  642.6 13.7 %copy-start.8 = (f32[4,10,256,1]{3,2,1,0:T(8,128)S(1)}, f32[4,10,256,1]{3,2,1,0:T(8,128)}, u32[]{:S(2)}) copy-start(f32[4,10,256,1]{3,2,1,0:T(8,128)} %copy.39) | copy-start | bytes 122884
  644.9 7.3 collective-permute-start.2
  650.3 6.0 collective-permute-start.3
  702.7 14.9 %copy-start.2 = (f32[10,258,514]{2,1,0:T(8,128)S(1)}, f32[10,258,514]{2,1,0:T(8,128)}, u32[]{:S(2)}) copy-start(f32[10,258,514]{2,1,0:T(8,128)} %get-tuple-element.14) | copy-start | bytes 15913444
  702.7 16.9 %copy-start.3 = (f32[10,258,514]{2,1,0:T(8,128)S(1)}, f32[10,258,514]{2,1,0:T(8,128)}, u32[]{:S(2)}) copy-start(f32[10,258,514]{2,1,0:T(8,128)} %get-tuple-element.15) | copy-start | bytes 15913444
  730.3 11.2 %copy-start.1 = (bf16[2048,512]{1,0:T(8,128)(2,1)S(1)}, bf16[2048,512]{1,0:T(8,128)(2,1)}, u32[]{:S(2)}) copy-start(bf16[2048,512]{1,0:T(8,128)(2,1)} %param.17) | copy-start | bytes 6291460
Sparse Core Ops, SparseCore 0:
  11.8 106.1 all-gather.5
  119.6 155.0 all-gather.7
  276.3 83.3 all-gather.9
  506.2 103.3 all-gather.11
where the time goes:
time: 755 us; the launch traced here: 748 us
  waiting for transfers between devices  221 us (29%)
  blocking collectives  188 us (25%)
  other arithmetic  165 us (22%)
  local copies, waits for them, and re-layouts  97.4 us (13%)
  matrix products  39.1 us (5%)
  between operations  19.7 us (3%)
  starting transfers between devices  18.2 us (2%)
    all_gather x1, blocking collectives, shards(): all_y = lax.all_gather(lambda_y, 'py', axis=0, tiled=True)  122 us
    all_gather x1, waiting for transfers between devices, shards(): lax.all_gather(rounded, 'px', axis=2, tiled=True)  105 us
    all_gather x1, waiting for transfers between devices, shards(): lax.all_gather(back_y, 'px', axis=2, tiled=True)  83.4 us
    all_to_all x1, blocking collectives, shards(): back_y = lax.all_to_all(back_pencil, 'py', 1, 2, tiled=True)  66.5 us
    unnamed x9, other arithmetic  54 us
    concatenate x1, other arithmetic, with_halo(): block = jnp.concatenate([low, block, high], axis=dim)  27.9 us
    all_to_all x1, waiting for transfers between devices, shards(): pencil = lax.all_to_all(spectral_x, 'py', 2, 1, tiled=True)  26.8 us
    unnamed x37, local copies, waits for them, and re-layouts  20.7 us
  transfers between devices with their start and end apart: 9, of which 5 were waited for; matrix products, arithmetic and copies ran while one was open for 17% of the time, Pallas kernels for 0%

commit v1 on v0

--- a/solution.py
+++ b/solution.py
@@ -82,7 +82,10 @@
         solved,
         preferred_element_type=jnp.float32,
     ).astype(jnp.bfloat16)
-    back_y = lax.all_to_all(back_pencil, "py", 1, 2, tiled=True)
+    back_y = jnp.concatenate(
+        lax.all_to_all(jnp.stack(jnp.split(back_pencil, lax.axis_size("py"), axis=1)), "py", 0, 0),
+        axis=2,
+    )
     del count_y
     mobility = jnp.zeros(regime_code.shape, jnp.float32)
     for regime in range(mobility_table.shape[0]):

time: 755 us -> 718 us (0.951)
  local copies, waits for them, and re-layouts: 97.4 us -> 62.2 us
    unnamed x37 -> x42, local copies, waits for them, and re-layouts: 20.7 us -> 3.11 us
    all_to_all x2 -> x0, local copies, waits for them, and re-layouts: 13.4 us -> none  [shards(): back_y = lax.all_to_all(back_pencil, 'py', 1, 2, tiled=True)]
    convert_element_type x1 -> x0, local copies, waits for them, and re-layouts: 10.4 us -> none  [shards(): back_pencil = jnp.einsum('yj,zji->zyi', lax.all_gather(right_y, 'py', axi...]
  transfers between devices with their start and end apart: 9 -> 9, of which waited for: 5 -> 5; matrix products, arithmetic and copies ran while one was open for 17% -> 18% of each run, Pallas kernels for 0% -> 0%
where the time goes in v1:
time: 718 us; the launch traced here: 712 us
  waiting for transfers between devices  221 us (31%)
  blocking collectives  187 us (26%)
  other arithmetic  165 us (23%)
  local copies, waits for them, and re-layouts  62.2 us (9%)
  matrix products  38.2 us (5%)
  between operations  19.8 us (3%)
  starting transfers between devices  18.2 us (3%)
    all_gather x1, blocking collectives, shards(): all_y = lax.all_gather(lambda_y, 'py', axis=0, tiled=True)  122 us
    all_gather x1, waiting for transfers between devices, shards(): lax.all_gather(rounded, 'px', axis=2, tiled=True)  105 us
    all_gather x1, waiting for transfers between devices, shards(): lax.all_gather(back_y, 'px', axis=2, tiled=True)  83.9 us
    all_to_all x1, blocking collectives, shards(): lax.all_to_all(jnp.stack(jnp.split(back_pencil, lax.axis_size('py'), axis...  65.4 us
    unnamed x9, other arithmetic  54 us
    concatenate x1, other arithmetic, with_halo(): block = jnp.concatenate([low, block, high], axis=dim)  27.9 us
    all_to_all x1, waiting for transfers between devices, shards(): pencil = lax.all_to_all(spectral_x, 'py', 2, 1, tiled=True)  26.8 us
    squeeze x1, local copies, waits for them, and re-layouts, shards(): flags_x = extended[2][:, 1:-1, :]  18.6 us
  transfers between devices with their start and end apart: 9, of which 5 were waited for; matrix products, arithmetic and copies ran while one was open for 18% of the time, Pallas kernels for 0%

profile of v1, /device:TPU:3, one launch (start us, length us, event | category | flops | bytes accessed | tf_op | source)
XLA Modules:
  0.0 712.0 jit_solution(6561292869936975260)
XLA Ops:
  7.2 4.5 convert_element_type.21
  13.2 104.8 %all-gather.6.cloned.1.call-done = bf16[10,256,2048]{2,1,0:T(8,128)(2,1)} async-done(((bf16[10,256,512]{2,1,0:T(8,128)(2,1)}), bf16[10,256,2048]{2,1,0:T(8,128)(2,1)}) %all-gather.6.cloned.1.call-update) | async-done | bytes 10485776 | tf_op jit(solution)/shard_map/all_gather | solution.py:64
  118.0 10.8 %fusion.22 = bf16[10,256,512]{2,1,0:T(8,128)(2,1)} fusion(bf16[10,256,2048]{2,1,0:T(8,128)(2,1)} %all-gather.6.cloned.1.call-done, bf16[2048,512]{1,0:T(8,128)(2,1)S(1)} %copy-done), kind=kOutput, calls=%fused_computation.46 | convolution fusion | flops 5370019840 | bytes 15204352 | tf_op jit(solution)/shard_map/zyx,xi->zyi/dot_general | solution.py:62
  128.9 7.6 %copy.19 = bf16[10,256,512]{1,0,2:T(8,128)(2,1)} copy(bf16[10,256,512]{2,1,0:T(8,128)(2,1)} %fusion.22) | data formatting | bytes 5242880 | tf_op jit(solution)/shard_map/convert_element_type | solution.py:67
  136.5 5.5 all-to-all-start
  149.0 121.9 %all-gather = f32[8,1,256]{2,1,0:T(1,128)S(1)} all-gather(f32[1,1,256]{2,1,0:T(1,128)S(1)} %bitcast.118), channel_id=1, replica_groups=mesh['px'=4,'py'=8] {'py'}, dimensions={0}, use_global_device_ids=true | all-gather | bytes 9216 | tf_op jit(solution)/shard_map/all_gather | solution.py:77
  271.5 26.8 %all-to-all-done = bf16[10,256,512]{1,0,2:T(8,128)(2,1)} async-done(((bf16[10,256,512]{1,0,2:T(8,128)(2,1)}), bf16[10,256,512]{1,0,2:T(8,128)(2,1)}, u32[]{:S(2)}, u32[]{:S(2)}) %all-to-all-start) | async-done | bytes 2621472 | tf_op jit(solution)/shard_map/all_to_all | solution.py:68
  298.4 5.3 copy.21
  303.7 5.7 all_to_all.19
  309.4 9.0 %fusion.9 = f32[10,2048,64]{1,2,0:T(8,128)S(1)} fusion(bf16[10,2048,64]{1,2,0:T(8,128)(2,1)} %all_to_all.19, bf16[2048,2048]{1,0:T(8,128)(2,1)} %all-gather.8.cloned.1.call-done), kind=kOutput, calls=%fused_computation.29 | convolution fusion | flops 5368709120 | bytes 16252928 | tf_op jit(solution)/shard_map/jy,zyi->zji/dot_general | solution.py:70
  318.4 14.9 %fusion.78 = (bf16[10,2048,64]{1,2,0:T(8,128)(2,1)}, bf16[1,2048,64]{1,2,0:T(8,128)(2,1)S(1)}, f32[1,2048,64]{1,2,0:T(8,128)S(1)}, f32[1,2048,64]{1,2,0:T(8,128)...) fusion(f32[]{:T(128)S(6)} %neg.27, f32[]{:T(128)} %bitcast.9, ...), kind=kLoop, calls=%fused_computation.126 | loop fusion | flops 13631487 | bytes 8921456
  334.1 4.8 convert_dynamic-update-slice_fusion.7
  339.6 7.6 %convert_dynamic-update-slice_fusion.5 = bf16[10,2048,64]{1,2,0:T(8,128)(2,1)} fusion(bf16[10,2048,64]{1,2,0:T(8,128)(2,1)} %convert_dynamic-update-slice_fusion.6, f32[1,2048,64]{1,2,0:T(8,128)S(1)} %get-tuple-element.8, f32[1,2048,64]{1,2,0:T(8,128)S(1)} %get-tuple-element.5, f32[]{:T(128)} %bitcast.8, f32[]{:T(128)S(6)} %neg.27, f32[]{:T(128)} %bitcast.9, ...), kind=kLoop, calls=%fused_computation.132 | loop fusion | flops 4063232 | bytes 1324308
  348.0 10.4 %convert_dynamic-update-slice_fusion.3 = bf16[10,2048,64]{1,2,0:T(8,128)(2,1)} fusion(bf16[10,2048,64]{1,2,0:T(8,128)(2,1)} %convert_dynamic-update-slice_fusion.4, f32[1,2048,64]{1,2,0:T(8,128)S(1)} %get-tuple-element.7, f32[1,2048,64]{1,2,0:T(8,128)S(1)} %get-tuple-element.6, f32[]{:T(128)} %bitcast.8, f32[]{:T(128)S(6)} %neg.27, f32[]{:T(128)} %bitcast.9, ...), kind=kLoop, calls=%fused_computation.130 | loop fusion | flops 5636096 | bytes 1326364
  359.1 14.0 %convert_dynamic-update-slice_fusion.1 = bf16[10,2048,64]{1,2,0:T(8,128)(2,1)} fusion(bf16[10,2048,64]{1,2,0:T(8,128)(2,1)} %convert_dynamic-update-slice_fusion.2, f32[]{:T(128)} %bitcast.8, f32[]{:T(128)S(6)} %neg.27, f32[]{:T(128)} %bitcast.9, f32[]{:T(128)} %bitcast.10, f32[]{:T(128)S(6)} %neg.28, f32[]{:T(128)} %bitcast.11, f32[]{:T(128)} %bitcast.12, ...), kind=kLoop, calls=%fused_computation.128 | loop fusion | flops 8912896 | bytes 2377508
  373.1 14.0 %convert_dynamic-update-slice_fusion = bf16[10,2048,64]{1,2,0:T(8,128)(2,1)} fusion(bf16[10,2048,64]{1,2,0:T(8,128)(2,1)} %convert_dynamic-update-slice_fusion.1, f32[]{:T(128)} %bitcast.8, f32[]{:T(128)S(6)} %neg.27, f32[]{:T(128)} %bitcast.9, f32[]{:T(128)} %bitcast.10, f32[]{:T(128)S(6)} %neg.28, f32[]{:T(128)} %bitcast.11, f32[]{:T(128)} %bitcast.12, ...), kind=kLoop, calls=%fused_computation.127 | loop fusion | flops 8650752 | bytes 2377508 | tf_op jit(solution)/shard_map/stack | solution.py:43
  387.1 9.8 %fusion.15 = bf16[10,2048,64]{1,2,0:T(8,128)(2,1)S(1)} fusion(bf16[10,2048,64]{1,2,0:T(8,128)(2,1)} %convert_dynamic-update-slice_fusion, bf16[2048,2048]{1,0:T(8,128)(2,1)} %all-gather.10.cloned.1.call-done), kind=kOutput, calls=%fused_computation.31 | convolution fusion | flops 5370019840 | bytes 13631488 | tf_op jit(solution)/shard_map/yj,zji->zyi/dot_general | solution.py:79
  397.4 65.4 %all_to_all.23 = bf16[8,10,256,64]{2,3,1,0:T(8,128)(2,1)S(1)} all-to-all(bf16[8,10,256,64]{2,3,1,0:T(8,128)(2,1)S(1)} %fusion.70), channel_id=1, replica_groups=mesh['px'=4,'py'=8] {'py'}, dimensions={0} | all-to-all | bytes 5242880 | tf_op jit(solution)/shard_map/all_to_all | solution.py:86
  464.6 4.4 copy.23
  469.7 9.2 %select_bitcast_fusion = f32[1,10,256,512]{3,2,1,0:T(8,128)} fusion(s32[10,256,512]{2,1,0:T(8,128)} %param.21, f32[]{:T(128)} %bitcast.44, f32[]{:T(128)} %bitcast.43, f32[]{:T(128)} %bitcast.42, f32[]{:T(128)} %bitcast.41), kind=kLoop, calls=%fused_computation.28 | loop fusion | flops 10485760 | bytes 10485776 | tf_op jit(solution)/shard_map/stack | solution.py:101
  478.9 10.5 %slice_convert_fusion.1 = (f32[1,10,256,512]{3,2,1,0:T(8,128)}, f32[1,10,256,512]{3,2,1,0:T(8,128)}) fusion(s32[2,10,256,512]{3,2,1,0:T(8,128)} %param.22), kind=kLoop, calls=%fused_computation.27 | loop fusion | flops 2621440 | bytes 20971520 | tf_op jit(solution)/shard_map/convert_element_type | solution.py:105
  489.4 83.9 %all-gather.12.cloned.1.call-done = bf16[10,256,2048]{2,1,0:T(8,128)(2,1)} async-done(((bf16[10,256,512]{2,1,0:T(8,128)(2,1)}), bf16[10,256,2048]{2,1,0:T(8,128)(2,1)}) %all-gather.12.cloned.1.call-update) | async-done | bytes 10485776 | tf_op jit(solution)/shard_map/all_gather | solution.py:95
  573.3 8.5 %fusion.18 = f32[10,256,512]{2,1,0:T(8,128)S(1)} fusion(bf16[10,256,2048]{2,1,0:T(8,128)(2,1)} %all-gather.12.cloned.1.call-done, bf16[2048,512]{1,0:T(8,128)(2,1)S(1)} %copy-done.14), kind=kOutput, calls=%fused_computation.42 | convolution fusion | flops 5368709120 | bytes 17825792 | tf_op jit(solution)/shard_map/zyi,ix->zyx/dot_general | solution.py:93
  581.8 5.9 pad_maximum_fusion.4
  594.2 3.3 copy.25
  608.6 5.4 collective-permute-start.2
  615.9 4.0 collective-permute-done.3
  619.9 27.9 %pad_maximum_fusion = f32[4,10,258,514]{3,2,1,0:T(8,128)} fusion(f32[4,10,1,514]{3,2,1,0:T(1,128)S(1)} %collective-permute-done.3, f32[4,10,256,1]{3,2,1,0:T(8,128)S(1)} %copy-done.8, f32[1,10,256,512]{3,2,1,0:T(8,128)} %get-tuple-element.19, f32[1,10,256,512]{3,2,1,0:T(8,128)S(1)} %bitcast.106, f32[1,10,256,512]{3,2,1,0:T(8,128)} %select_bitcast_fusion, ...), kind=kLoop, calls=%fused_computation | loop fusion | flops 37131360 | bytes 42435840 | tf_op jit(solution)/shard_map/concatenate | solution.py:16
  647.8 18.6 %slice_bitcast_fusion.3 = (f32[10,258,514]{2,1,0:T(8,128)}, f32[10,258,514]{2,1,0:T(8,128)}, f32[10,258,514]{2,1,0:T(8,128)}, f32[10,258,514]{2,1,0:T(8,128)}) fusion(f32[4,10,258,514]{3,2,1,0:T(8,128)} %pad_maximum_fusion), kind=kLoop, calls=%fused_computation.8 | loop fusion | bytes 42435840 | tf_op jit(solution)/shard_map/squeeze | solution.py:112
  666.4 14.9 %fusion.5 = f32[10,256,513]{2,1,0:T(8,128)} fusion(f32[10,258,514]{2,1,0:T(8,128)} %get-tuple-element.14, f32[10,258,514]{2,1,0:T(8,128)} %get-tuple-element.15, f32[10,258,514]{2,1,0:T(8,128)} %get-tuple-element.12, pred[513]{0:T(1024)(128)(4,1)S(1)} %fusion.81), kind=kLoop, calls=%fused_computation.11 | loop fusion | flops 6566400 | bytes 31519232 | tf_op jit(solution)/shard_map/jit(_where)/select_n | solution.py:117
  683.2 10.7 %fusion.7 = f32[10,257,512]{2,1,0:T(8,128)} fusion(f32[10,258,514]{2,1,0:T(8,128)S(1)} %copy-done.2, f32[10,258,514]{2,1,0:T(8,128)S(1)} %copy-done.3, f32[10,258,514]{2,1,0:T(8,128)} %get-tuple-element.13, pred[257]{0:T(512)(128)(4,1)S(1)} %fusion.84), kind=kLoop, calls=%fused_computation.16 | loop fusion | flops 6579200 | bytes 31580416 | tf_op jit(solution)/shard_map/jit(_where)/select_n | solution.py:126
  694.0 11.2 %fusion.8 = f32[10,256,512]{2,1,0:T(8,128)} fusion(f32[10,257,512]{2,1,0:T(8,128)} %fusion.7, f32[10,256,513]{2,1,0:T(8,128)} %fusion.5), kind=kLoop, calls=%fused_computation.20 | loop fusion | flops 3932160 | bytes 26214400 | tf_op jit(solution)/shard_map/add | solution.py:128
  (74 shorter events, 30.8 us)
Async XLA Ops:
  7.2 110.8 %copy-start = (bf16[2048,512]{1,0:T(8,128)(2,1)S(1)}, bf16[2048,512]{1,0:T(8,128)(2,1)}, u32[]{:S(2)}) copy-start(bf16[2048,512]{1,0:T(8,128)(2,1)} %param.17) | copy-start | bytes 6291460
  7.2 110.8 %all-gather.6.cloned.1.call-start = ((), (), s32[]{:S(2)}) async-start(), calls=%async_computation.2 | async-start | bytes 13107200 | tf_op jit(solution)/shard_map/all_gather | solution.py:64
  11.7 297.7 %all-gather.8.cloned.1.call-start = ((), (), s32[]{:S(2)}) async-start(), calls=%async_computation.3 | async-start | bytes 9437184 | tf_op jit(solution)/shard_map/all_gather | solution.py:72
  12.5 374.6 %all-gather.10.cloned.1.call-start = ((), (), s32[]{:S(2)}) async-start(), calls=%async_computation.4 | async-start | bytes 9437184 | tf_op jit(solution)/shard_map/all_gather | solution.py:81
  136.5 5.5 copy-start.11
  136.5 12.5 %copy-start.13 = (f32[256]{0:T(256)S(1)}, f32[256]{0:T(256)}, u32[]{:S(2)}) copy-start(f32[256]{0:T(256)} %param.14) | copy-start | bytes 3076
  136.5 134.4 %copy-start.10 = (f32[10]{0:T(128)S(1)}, f32[10]{0:T(128)}, u32[]{:S(2)}) copy-start(f32[10]{0:T(128)} %param.16) | copy-start | bytes 124
  136.5 161.9 %all-to-all-start = ((bf16[10,256,512]{1,0,2:T(8,128)(2,1)}), bf16[10,256,512]{1,0,2:T(8,128)(2,1)}, u32[]{:S(2)}, u32[]{:S(2)}) async-start(bf16[10,256,512]{1,0,2:T(8,128)(2,1)} %copy.19), calls=%async_computation | async-start | bytes 8388608 | tf_op jit(solution)/shard_map/all_to_all | solution.py:68
  142.0 431.3 %all-gather.12.cloned.1.call-start = ((), (), s32[]{:S(2)}) async-start(), calls=%async_computation.5 | async-start | bytes 13107200 | tf_op jit(solution)/shard_map/all_gather | solution.py:95
  464.6 4.4 copy-start.12
  478.9 94.4 %copy-start.14 = (bf16[2048,512]{1,0:T(8,128)(2,1)S(1)}, bf16[2048,512]{1,0:T(8,128)(2,1)}, u32[]{:S(2)}) copy-start(bf16[2048,512]{1,0:T(8,128)(2,1)} %param.20) | copy-start | bytes 6291460
  573.3 8.5 %copy-start.4 = (f32[1,10,256,512]{3,2,1,0:T(8,128)S(1)}, f32[1,10,256,512]{3,2,1,0:T(8,128)}, u32[]{:S(2)}) copy-start(f32[1,10,256,512]{3,2,1,0:T(8,128)} %get-tuple-element.18) | copy-start | bytes 15728644
  573.3 8.5 %copy-start.5 = (f32[1,10,256,512]{3,2,1,0:T(8,128)S(1)}, f32[1,10,256,512]{3,2,1,0:T(8,128)}, u32[]{:S(2)}) copy-start(f32[1,10,256,512]{3,2,1,0:T(8,128)} %get-tuple-element.19) | copy-start | bytes 15728644
  573.3 8.6 %copy-start.6 = (f32[1,10,256,512]{3,2,1,0:T(8,128)S(1)}, f32[1,10,256,512]{3,2,1,0:T(8,128)}, u32[]{:S(2)}) copy-start(f32[1,10,256,512]{3,2,1,0:T(8,128)} %select_bitcast_fusion) | copy-start | bytes 15728644
  581.7 6.0 copy-start.9
  591.1 8.6 %collective-permute-start = (f32[4,10,256,1]{2,0,3,1:T(4,128)S(1)}, f32[4,10,256,1]{2,0,3,1:T(4,128)S(1)}, u32[]{:S(2)}, u32[]{:S(2)}) collective-permute-start(f32[4,10,256,1]{2,0,3,1:T(4,128)S(1)} %copy.24), channel_id=1, source_target_pairs={{0,8},{8,16},{16,24},{1,9},{9,17},{17,25},{2,10},{10,18},{18,26},{... | collective-permute-start | bytes 122888 | tf_op jit(solution)/shard_map/ppermute | solution.py:12
  597.5 5.6 collective-permute-start.1
  603.2 16.8 %slice-start = ((s8[5242880]{0:T(1024)(128)(4,1)}), s8[1048576]{0:T(1024)(128)(4,1)S(1)}, s32[]{:S(2)}) async-start(s8[5242880]{0:T(1024)(128)(4,1)} %bitcast.105), calls=%async_computation.6 | async-start | bytes 2097152
  606.2 13.7 %slice-start.1 = ((s8[5242880]{0:T(1024)(128)(4,1)}), s8[4194304]{0:T(1024)(128)(4,1)S(1)}, s32[]{:S(2)}) async-start(s8[5242880]{0:T(1024)(128)(4,1)} %bitcast.105), calls=%async_computation.7 | async-start | bytes 8388608
  606.2 13.7 %copy-start.7 = (f32[4,10,256,1]{3,2,1,0:T(8,128)S(1)}, f32[4,10,256,1]{3,2,1,0:T(8,128)}, u32[]{:S(2)}) copy-start(f32[4,10,256,1]{3,2,1,0:T(8,128)} %copy.26) | copy-start | bytes 122884
  606.2 13.7 %copy-start.8 = (f32[4,10,256,1]{3,2,1,0:T(8,128)S(1)}, f32[4,10,256,1]{3,2,1,0:T(8,128)}, u32[]{:S(2)}) copy-start(f32[4,10,256,1]{3,2,1,0:T(8,128)} %copy.27) | copy-start | bytes 122884
  608.6 7.3 %collective-permute-start.2 = (f32[4,10,1,514]{3,2,1,0:T(1,128)S(1)}, f32[4,10,1,514]{3,2,1,0:T(1,128)S(1)}, u32[]{:S(2)}, u32[]{:S(2)}) collective-permute-start(f32[4,10,1,514]{3,2,1,0:T(1,128)S(1)} %get-tuple-element.10), channel_id=1, source_target_pairs={{0,1},{1,2},{2,3},{3,4},{4,5},{5,6},{6,7},{8,9},{9,10},{10,11},{11... | collective-permute-start | bytes 246728 | tf_op jit(solution)/shard_map/ppermute | solution.py:12
  613.9 6.0 collective-permute-start.3
  666.4 14.9 %copy-start.2 = (f32[10,258,514]{2,1,0:T(8,128)S(1)}, f32[10,258,514]{2,1,0:T(8,128)}, u32[]{:S(2)}) copy-start(f32[10,258,514]{2,1,0:T(8,128)} %get-tuple-element.14) | copy-start | bytes 15913444
  666.4 16.9 %copy-start.3 = (f32[10,258,514]{2,1,0:T(8,128)S(1)}, f32[10,258,514]{2,1,0:T(8,128)}, u32[]{:S(2)}) copy-start(f32[10,258,514]{2,1,0:T(8,128)} %get-tuple-element.15) | copy-start | bytes 15913444
  694.0 11.2 %copy-start.1 = (bf16[2048,512]{1,0:T(8,128)(2,1)S(1)}, bf16[2048,512]{1,0:T(8,128)(2,1)}, u32[]{:S(2)}) copy-start(bf16[2048,512]{1,0:T(8,128)(2,1)} %param.17) | copy-start | bytes 6291460
Sparse Core Ops, SparseCore 0:
  11.8 106.1 all-gather.5
  119.6 155.0 all-gather.7
  276.3 83.3 all-gather.9
  469.1 104.0 all-gather.11
